TPU v7x, 32 devices: a whole 2x2x4 slice. The times are simulated.
32 devices in a mesh: seq: 8 (over z, x), exp: 4 (over y, core).
Axes of the slice: x: 2, y: 2, z: 4, core: 2. Of those that a mesh axis runs over, the one named last changes fastest.
Arguments:
- hidden_in: bfloat16 [2048, 1536], P('seq'), may hold values from -6 to 6
- attn_gain: float32 [1536], replicated, may hold values from 0.1 to 1.9
- q_weight: bfloat16 [1536, 1536], P(None, 'exp'), may hold values from -1.25 to 1.25
- k_weight: bfloat16 [1536, 512], P(None, 'exp'), may hold values from -0.625 to 0.625
- v_weight: bfloat16 [1536, 512], P(None, 'exp'), may hold values from -0.15625 to 0.15625
- o_weight: bfloat16 [1536, 1536], P('exp'), may hold values from -0.15625 to 0.15625
- cache_kv: bfloat16 [4096, 1024], P('seq', 'exp'), may hold values from -216 to 216
- moe_gain: float32 [1536], replicated, may hold values from 0.1 to 1.9
- expert_in: bfloat16 [32, 1536, 1024], P('seq'), may hold values from -0.15625 to 0.15625
- expert_out: bfloat16 [32, 512, 1536], P('seq'), may hold values from -0.25 to 0.25
- routes: int32 [2048, 8], P(('seq', 'exp')), may hold values from 0 to 31, all different within a row; in each aligned block of 64 rows (0 to 63, 64 to 127, ...) at most 32 rows name the same one
- route_prob: float32 [2048, 8], P(('seq', 'exp')), may hold values from 0.05 to 1
- page_slot: int32 [256], replicated, may hold values from 0 to 31, as said below
Outputs:
- hidden_out: bfloat16 [2048, 1536], P(('seq', 'exp'))
- decode_pages: bfloat16 [256, 8, 2, 512], P('seq', 'exp')
Inputs may be any that keep to these rules, and one draw needn't show every extreme that they name: `routes`: in each aligned block of 64 rows (the rows of one device) no expert is named by more than 32 rows; a row names 8 different experts. `page_slot`: for each r, the 32 blocks b with b mod (8) == r have different slots.
All inputs are finite; a program needn't handle non-finite values.
Results may differ from a plain program's by a relative error of at most 0.0074.
Values may be sent and summed in bfloat16 or wider, within the bound.
No kernel may reach another device: no remote copies, remote signals or barrier semaphores. Data moves between devices by JAX's collectives and lax.ppermute only.
A program may use at most 128 MiB of HBM per device.

v0:
```python
import math
import jax
import jax.numpy as jnp
from jax import lax
from jax.sharding import PartitionSpec as P

HEADS = 24
KV_HEADS = 8
HEAD_DIM = 64
EXPERTS = 32
PAGE = 8
norm_epsilon = 1e-06
attention_scale = 0.015625
residual_scale = 0.22
masked_score = -1e30


def rms_norm(values, gain_row):
    widened = values.astype(jnp.float32)
    spread = lax.rsqrt(jnp.mean(widened * widened, axis=-1, keepdims=True) + norm_epsilon)
    return (widened * spread * gain_row).astype(jnp.bfloat16)


def attend_block(carried, query_heads, visible, key_rows, value_rows):
    best_old, total_old, summed_old = carried
    scores = (
        jnp.einsum("tkgd,nkd->kgtn", query_heads, key_rows, preferred_element_type=jnp.float32)
        * attention_scale
    )
    scores = jnp.where(visible, scores, masked_score)
    best_new = jnp.maximum(best_old, jnp.max(scores, axis=-1))
    weights = jnp.where(visible, jnp.exp(scores - best_new[..., None]), 0.0)
    factor = jnp.exp(best_old - best_new)
    total_new = total_old * factor + jnp.sum(weights, axis=-1)
    summed_new = summed_old * factor[..., None] + jnp.einsum(
        "kgtn,nkd->kgtd",
        weights.astype(jnp.bfloat16),
        value_rows,
        preferred_element_type=jnp.float32,
    )
    return (best_new, total_new, summed_new)


def block_size(piece_rows):
    return math.gcd(piece_rows, 512)


def body(
    hidden_in,
    attn_gain,
    q_weight,
    k_weight,
    v_weight,
    o_weight,
    cache_kv,
    moe_gain,
    expert_in,
    expert_out,
    routes,
    route_prob,
    page_slot,
):
    seq_count = lax.axis_size("seq")
    seq_index = lax.axis_index("seq")
    exp_index = lax.axis_index("exp")
    tokens_here = hidden_in.shape[0]
    head_dim = HEAD_DIM
    kv_local = k_weight.shape[1] // head_dim
    group_size = HEADS // KV_HEADS
    prompt_len = tokens_here * seq_count // 2
    first_row = seq_index * tokens_here
    query_rows = first_row + jnp.arange(tokens_here, dtype=jnp.int32)
    query_second = query_rows >= prompt_len
    holds_first = first_row < prompt_len
    normed = rms_norm(hidden_in, attn_gain)
    queries = jnp.dot(normed, q_weight, preferred_element_type=jnp.float32).astype(jnp.bfloat16)
    keys_new = jnp.dot(normed, k_weight, preferred_element_type=jnp.float32).astype(jnp.bfloat16)
    values_new = jnp.dot(normed, v_weight, preferred_element_type=jnp.float32).astype(jnp.bfloat16)
    pair_width = 2 * kv_local * head_dim
    pairs_new = jnp.stack(
        [
            keys_new.reshape(tokens_here, kv_local, head_dim),
            values_new.reshape(tokens_here, kv_local, head_dim),
        ],
        axis=2,
    ).reshape(tokens_here, pair_width)
    query_heads = queries.reshape(tokens_here, kv_local, group_size, head_dim)
    cache_lines = cache_kv.reshape(tokens_here, -1)
    blocks_here = tokens_here // PAGE
    rounds = blocks_here // seq_count
    outgoing = pairs_new.reshape(rounds, seq_count, PAGE * pair_width)
    received = lax.all_to_all(outgoing, "seq", split_axis=1, concat_axis=1, tiled=True)
    block_ids = (
        jnp.arange(seq_count, dtype=jnp.int32)[None, :] * blocks_here
        + jnp.arange(rounds, dtype=jnp.int32)[:, None] * seq_count
        + seq_index
    ).reshape(-1)
    table_ids = jnp.arange(page_slot.shape[0], dtype=jnp.int32)
    page_slots = jnp.sum(
        jnp.where(block_ids[:, None] == table_ids[None, :], page_slot[None, :], 0), axis=1
    )
    local_pages = (
        jnp.zeros((blocks_here, PAGE * pair_width), jnp.bfloat16)
        .at[page_slots]
        .set(received.reshape(blocks_here, -1))
    )
    page_rows = local_pages.reshape(blocks_here, PAGE, kv_local, 2, head_dim).transpose(
        0, 2, 3, 1, 4
    )
    page_rows = page_rows.reshape(blocks_here, kv_local, 2, PAGE * head_dim)
    start_state = (
        jnp.full((kv_local, group_size, tokens_here), masked_score, jnp.float32),
        jnp.zeros((kv_local, group_size, tokens_here), jnp.float32),
        jnp.zeros((kv_local, group_size, tokens_here, head_dim), jnp.float32),
    )

    def new_keys_part(carried, new_block, key_first):
        width_rows = new_block.shape[0]
        key_rows = key_first + jnp.arange(width_rows, dtype=jnp.int32)
        visible = ((key_rows >= prompt_len)[None, :] == query_second[:, None]) & (
            key_rows[None, :] <= query_rows[:, None]
        )
        split_pairs = new_block.reshape(width_rows, kv_local, 2, head_dim)
        return lax.cond(
            jnp.any(visible),
            lambda carried_in: attend_block(
                carried_in, query_heads, visible, split_pairs[:, :, 0], split_pairs[:, :, 1]
            ),
            lambda carried_in: carried_in,
            carried,
        )

    carried = start_state
    new_piece = lax.all_gather(pairs_new, "seq", axis=0, tiled=True)
    cache_piece = lax.all_gather(cache_lines, "seq", axis=0, tiled=True)
    piece_rows = new_piece.shape[0]
    stride = block_size(piece_rows)
    new_blocks = new_piece.reshape(piece_rows // stride, stride, -1)
    cache_blocks = cache_piece.reshape(piece_rows // stride, 2 * stride, kv_local, 2, head_dim)
    offsets = stride * jnp.arange(piece_rows // stride, dtype=jnp.int32)
    everything = jnp.ones((tokens_here, 2 * stride), bool)

    def visit(carried_in, block_part):
        new_block, cache_block, key_first = block_part
        carried_in = new_keys_part(carried_in, new_block, key_first)
        carried_in = lax.cond(
            holds_first,
            lambda inner: attend_block(
                inner, query_heads, everything, cache_block[:, :, 0], cache_block[:, :, 1]
            ),
            lambda inner: inner,
            carried_in,
        )
        return (carried_in, None)

    carried, _ = lax.scan(visit, carried, (new_blocks, cache_blocks, offsets))
    best_final, total_final, summed_final = carried
    attended = (
        (summed_final / total_final[..., None])
        .transpose(2, 0, 1, 3)
        .reshape(tokens_here, -1)
        .astype(jnp.bfloat16)
    )
    mixed_rows = lax.psum_scatter(
        jnp.dot(attended, o_weight, preferred_element_type=jnp.float32).astype(jnp.bfloat16),
        "exp",
        scatter_dimension=0,
        tiled=True,
    ).astype(jnp.float32)
    moe_rows = mixed_rows.shape[0]
    residual = (
        lax.dynamic_slice_in_dim(hidden_in, exp_index * moe_rows, moe_rows, 0).astype(jnp.float32)
        + residual_scale * mixed_rows
    )
    moe_in = rms_norm(residual, moe_gain)
    top_count = routes.shape[1]
    assigns = moe_rows * top_count
    capacity = 2 * moe_rows * top_count // EXPERTS
    flat_ids = routes.reshape(-1)
    hit_table = (flat_ids[:, None] == jnp.arange(EXPERTS, dtype=jnp.int32)[None, :]).astype(
        jnp.int32
    )
    earlier = jnp.cumsum(hit_table, axis=0) - hit_table
    slot_rank = jnp.sum(earlier * hit_table, axis=1)
    dest_slot = flat_ids * capacity + slot_rank
    source = (
        jnp.full((EXPERTS * capacity,), assigns, jnp.int32)
        .at[dest_slot]
        .set(jnp.arange(assigns, dtype=jnp.int32))
    )
    filled = source < assigns
    picked = moe_in[jnp.minimum(source, assigns - 1) // top_count]
    dispatched = jnp.where(filled[:, None], picked, jnp.zeros_like(picked)).reshape(
        seq_count, EXPERTS // seq_count, capacity, -1
    )
    hidden = jnp.einsum(
        "sexd,edf->sexf",
        lax.all_to_all(dispatched, "seq", split_axis=0, concat_axis=0, tiled=True),
        expert_in,
        preferred_element_type=jnp.float32,
    )
    half_width = hidden.shape[-1] // 2
    active = (jax.nn.silu(hidden[..., :half_width]) * hidden[..., half_width:]).astype(jnp.bfloat16)
    produced = jnp.einsum(
        "sexf,efd->sexd", active, expert_out, preferred_element_type=jnp.float32
    ).astype(jnp.bfloat16)
    returned = lax.all_to_all(produced, "seq", split_axis=0, concat_axis=0, tiled=True)
    flat_back = returned.reshape(EXPERTS * capacity, -1)
    per_assign = flat_back[dest_slot].reshape(moe_rows, top_count, -1)
    share = route_prob / jnp.sum(route_prob, axis=-1, keepdims=True)
    moe = jnp.sum(share[..., None] * per_assign.astype(jnp.float32), axis=1)
    hidden_out = (residual + residual_scale * moe).astype(jnp.bfloat16)
    return (hidden_out, page_rows)


def solution(mesh):
    return jax.shard_map(
        body,
        mesh=mesh,
        in_specs=(
            P("seq", None),
            P(),
            P(None, "exp"),
            P(None, "exp"),
            P(None, "exp"),
            P("exp", None),
            P("seq", "exp"),
            P(),
            P("seq", None, None),
            P("seq", None, None),
            P(("seq", "exp"), None),
            P(("seq", "exp"), None),
            P(),
        ),
        out_specs=(P(("seq", "exp"), None), P("seq", "exp", None, None)),
        check_vma=False,
    )
```

profile of v0, /device:TPU:0, one launch (start us, length us, event | category | flops | bytes accessed | tf_op | source)
XLA Modules:
  0.0 385.0 jit_solution(13722507623709581729)
XLA Ops:
  7.3 1.5 fusion.45
  8.8 1.7 convolution_convert_fusion.3
  10.5 1.7 convolution_convert_fusion.2
  13.0 0.8 reshape.172
  14.7 40.6 %all-gather.3.cloned.1.call-done = bf16[2048,256]{0,1:T(8,128)(2,1)} async-done(((bf16[256,256]{0,1:T(8,128)(2,1)}), bf16[2048,256]{0,1:T(8,128)(2,1)}) %all-gather.3.cloned.1.call-update) | async-done | bytes 1048592 | tf_op jit(solution)/shard_map/all_gather | solution.py:134
  55.4 1.3 copy.142
  56.7 49.0 %all-gather.5.cloned.1.call-done = bf16[2048,512]{1,0:T(8,128)(2,1)} async-done(((bf16[256,512]{1,0:T(8,128)(2,1)}), bf16[2048,512]{1,0:T(8,128)(2,1)}) %all-gather.5.cloned.1.call-update) | async-done | bytes 2097168 | tf_op jit(solution)/shard_map/all_gather | solution.py:135
  105.7 8.9 %reshape.173 = bf16[4,1024,2,2,64]{4,3,2,1,0:T(2,128)(2,1)} reshape(bf16[2048,512]{1,0:T(8,128)(2,1)} %all-gather.5.cloned.1.call-done) | data formatting | bytes 4194304 | tf_op jit(solution)/shard_map/reshape | solution.py:139
  114.6 10.6 %copy.101 = bf16[4,1024,2,2,64]{1,4,2,3,0:T(8,128)(2,1)} copy(bf16[4,1024,2,2,64]{4,3,2,1,0:T(2,128)(2,1)} %reshape.173) | data formatting | bytes 4194304
  125.3 35.4 %while.16 = (s32[]{:T(128)}, f32[2,3,256]{2,1,0:T(4,128)S(1)}, f32[2,3,256]{2,1,0:T(4,128)S(1)}, f32[2,3,256,64]{2,3,1,0:T(8,128)S(1)}, pred[]{:T(512)}, /*index...) while((s32[]{:T(128)}, f32[2,3,256]{2,1,0:T(4,128)S(1)}, ...), condition=%wide.region_11.12_spmd.clone.clone, body=%wide.region_1.11_spmd.clone.clone.sunk | while | flops 627712256 | bytes 33374036 | solution.py:156
  126.7 0.7 broadcast_compare_fusion.6
  127.4 0.9 fusion.79
  129.0 2.5 conditional.8
  129.7 0.8 fusion.6
  130.5 1.0 fusion.10
  131.5 4.5 %conditional.9 = ((f32[2,3,256]{2,1,0:T(4,128)S(1)}, f32[2,3,256]{2,1,0:T(4,128)S(1)}, f32[2,3,256,64]{2,3,1,0:T(8,128)S(1)})) conditional(s32[]{:T(128)} %convert_element_type.152, (f32[2,3,256]{2,1,0:T(4,128)S(1)}, f32[2,3,256]{2,1,0:T(4,128)S(1)}, f32[2,3,256,64]{2,3,1,0:T(8,128)S(1)}) %get-tuple-element.445, ...), branch_computations={%region_7.7_spmd, %region_8.10_spmd} | conditional | flops 415435776 | bytes 21532708 | solution.py:146
  131.5 1.1 dynamic-slice_bitcast_fusion
  132.6 1.0 bitcast_reduce_fusion
  133.7 1.0 fusion.19
  134.7 1.2 fusion.22
  137.4 0.7 broadcast_compare_fusion.6
  138.1 0.9 fusion.79
  139.7 4.5 %conditional.9 = ((f32[2,3,256]{2,1,0:T(4,128)S(1)}, f32[2,3,256]{2,1,0:T(4,128)S(1)}, f32[2,3,256,64]{2,3,1,0:T(8,128)S(1)})) conditional(s32[]{:T(128)} %convert_element_type.152, (f32[2,3,256]{2,1,0:T(4,128)S(1)}, f32[2,3,256]{2,1,0:T(4,128)S(1)}, f32[2,3,256,64]{2,3,1,0:T(8,128)S(1)}) %get-tuple-element.445, ...), branch_computations={%region_7.7_spmd, %region_8.10_spmd} | conditional | flops 415435776 | bytes 21532708 | solution.py:146
  139.8 1.1 dynamic-slice_bitcast_fusion
  140.8 1.0 bitcast_reduce_fusion
  141.9 1.0 fusion.19
  143.0 1.2 fusion.22
  145.6 0.7 broadcast_compare_fusion.6
  146.3 0.9 fusion.79
  148.0 4.5 %conditional.9 = ((f32[2,3,256]{2,1,0:T(4,128)S(1)}, f32[2,3,256]{2,1,0:T(4,128)S(1)}, f32[2,3,256,64]{2,3,1,0:T(8,128)S(1)})) conditional(s32[]{:T(128)} %convert_element_type.152, (f32[2,3,256]{2,1,0:T(4,128)S(1)}, f32[2,3,256]{2,1,0:T(4,128)S(1)}, f32[2,3,256,64]{2,3,1,0:T(8,128)S(1)}) %get-tuple-element.445, ...), branch_computations={%region_7.7_spmd, %region_8.10_spmd} | conditional | flops 415435776 | bytes 21532708 | solution.py:146
  148.0 1.1 dynamic-slice_bitcast_fusion
  149.1 1.0 bitcast_reduce_fusion
  150.1 1.0 fusion.19
  151.2 1.2 fusion.22
  153.8 0.7 broadcast_compare_fusion.6
  154.6 0.9 fusion.79
  156.2 4.5 %conditional.9 = ((f32[2,3,256]{2,1,0:T(4,128)S(1)}, f32[2,3,256]{2,1,0:T(4,128)S(1)}, f32[2,3,256,64]{2,3,1,0:T(8,128)S(1)})) conditional(s32[]{:T(128)} %convert_element_type.152, (f32[2,3,256]{2,1,0:T(4,128)S(1)}, f32[2,3,256]{2,1,0:T(4,128)S(1)}, f32[2,3,256,64]{2,3,1,0:T(8,128)S(1)}) %get-tuple-element.445, ...), branch_computations={%region_7.7_spmd, %region_8.10_spmd} | conditional | flops 415435776 | bytes 21532708 | solution.py:146
  156.2 1.1 dynamic-slice_bitcast_fusion
  157.3 1.0 bitcast_reduce_fusion
  158.4 1.0 fusion.19
  159.4 1.2 fusion.22
  160.8 1.5 convolution_convert_fusion
  162.6 1.2 reduce-window.6
  164.3 2.4 scatter_custom_fusion
  166.9 19.4 %reduce-scatter.2.cloned.1.call-done = bf16[64,1536]{1,0:T(8,128)(2,1)} async-done(((bf16[256,1536]{1,0:T(8,128)(2,1)}), bf16[64,1536]{1,0:T(8,128)(2,1)}) %reduce-scatter.2.cloned.1.call-update) | async-done | bytes 196624 | tf_op jit(solution)/shard_map/reduce_scatter | solution.py:164
  186.3 1.1 multiply_reduce_fusion
  187.4 1.0 multiply_convert_fusion
  188.5 5.6 %gather_fusion = bf16[1024,1536]{1,0:T(8,128)(2,1)} fusion(bf16[64,1536]{1,0:T(8,128)(2,1)S(1)} %multiply_convert_fusion, s32[1024]{0:T(1024)S(1)} %fusion.59), kind=kCustom, calls=%fused_computation | custom fusion | bytes 6295552 | tf_op jit(solution)/shard_map/gather | solution.py:192
  194.1 3.8 broadcast_select_fusion
  197.9 5.8 %all-to-all-start = ((bf16[8,4,32,1536]{3,2,1,0:T(8,128)(2,1)}), bf16[8,4,32,1536]{3,2,1,0:T(8,128)(2,1)}, u32[]{:S(2)}, u32[]{:S(2)}) async-start(bf16[8,4,32,1536]{3,2,1,0:T(8,128)(2,1)} %broadcast_select_fusion), calls=%async_computation.1 | async-start | bytes 6291456 | tf_op jit(solution)/shard_map/all_to_all | solution.py:198
  204.2 0.8 copy.110
  204.9 69.6 %all-to-all-done = bf16[8,4,32,1536]{3,2,1,0:T(8,128)(2,1)} async-done(((bf16[8,4,32,1536]{3,2,1,0:T(8,128)(2,1)}), bf16[8,4,32,1536]{3,2,1,0:T(8,128)(2,1)}, u32[]{:S(2)}, u32[]{:S(2)}) %all-to-all-start) | async-done | bytes 3145760 | tf_op jit(solution)/shard_map/all_to_all | solution.py:198
  274.5 3.6 all-to-all-start.2
  278.2 7.4 %fusion.39 = f32[8,4,32,1024]{3,2,0,1:T(8,128)S(1)} fusion(bf16[4,1536,1024]{2,1,0:T(8,128)(2,1)} %param.27, bf16[8,4,32,1536]{3,2,1,0:T(8,128)(2,1)} %all-to-all-done), kind=kOutput, calls=%fused_computation.53 | convolution fusion | flops 3221225472 | bytes 19922944 | tf_op jit(solution)/shard_map/sexd,edf->sexf/dot_general | solution.py:196
  285.6 4.6 %fusion.34 = bf16[8,4,32,1536]{3,2,0,1:T(8,128)(2,1)S(1)} fusion(bf16[4,512,1536]{2,1,0:T(8,128)(2,1)} %param.28, f32[8,4,32,1024]{3,2,0,1:T(8,128)S(1)} %fusion.39), kind=kOutput, calls=%fused_computation.47 | convolution fusion | flops 1615331328 | bytes 13631488 | tf_op jit(solution)/shard_map/sexf,efd->sexd/dot_general | solution.py:204
  290.2 1.9 copy.108
  292.1 6.1 %all-to-all-start.1 = ((bf16[8,4,32,1536]{3,2,1,0:T(8,128)(2,1)}), bf16[8,4,32,1536]{3,2,1,0:T(8,128)(2,1)}, u32[]{:S(2)}, u32[]{:S(2)}) async-start(bf16[8,4,32,1536]{3,2,1,0:T(8,128)(2,1)} %copy.108), calls=%async_computation.2 | async-start | bytes 6291456 | tf_op jit(solution)/shard_map/all_to_all | solution.py:207
  298.3 0.7 copy.102
  299.3 0.9 scatter_custom_fusion.1
  300.5 0.8 reshape.221
  301.4 67.3 %all-to-all-done.1 = bf16[8,4,32,1536]{3,2,1,0:T(8,128)(2,1)} async-done(((bf16[8,4,32,1536]{3,2,1,0:T(8,128)(2,1)}), bf16[8,4,32,1536]{3,2,1,0:T(8,128)(2,1)}, u32[]{:S(2)}, u32[]{:S(2)}) %all-to-all-start.1) | async-done | bytes 3145760 | tf_op jit(solution)/shard_map/all_to_all | solution.py:207
  368.7 5.9 %gather_fusion.1 = bf16[512,1536]{1,0:T(8,128)(2,1)S(1)} fusion(bf16[1024,1536]{1,0:T(8,128)(2,1)} %bitcast.33, s32[1024]{0:T(1024)S(1)} %pad_clamp_fusion), kind=kCustom, calls=%fused_computation.1 | custom fusion | bytes 3147776 | tf_op jit(solution)/shard_map/gather | solution.py:209
  374.6 2.2 fusion.37
  376.8 1.7 add_convert_fusion
  (107 shorter events, 10.2 us)
Async XLA Ops:
  7.2 153.6 %copy-start = (bf16[384,1536]{1,0:T(8,128)(2,1)S(1)}, bf16[384,1536]{1,0:T(8,128)(2,1)}, u32[]{:S(2)}) copy-start(bf16[384,1536]{1,0:T(8,128)(2,1)} %param.24) | copy-start | bytes 3538948
  7.2 6.7 %copy-start.1 = (bf16[256,1536]{1,0:T(8,128)(2,1)S(1)}, bf16[256,1536]{1,0:T(8,128)(2,1)}, u32[]{:S(2)}) copy-start(bf16[256,1536]{1,0:T(8,128)(2,1)} %param.19) | copy-start | bytes 2359300
  7.2 6.7 %copy-start.10 = (f32[1536]{0:T(1024)S(1)}, f32[1536]{0:T(1024)}, u32[]{:S(2)}) copy-start(f32[1536]{0:T(1024)} %param.20) | copy-start | bytes 18436
  7.2 5.8 %copy-start.4 = (bf16[512,256]{1,0:T(8,128)(2,1)S(1)}, bf16[512,256]{1,0:T(8,128)(2,1)}, u32[]{:S(2)}) copy-start(bf16[512,256]{1,0:T(8,128)(2,1)} %param.25) | copy-start | bytes 786436
  7.2 6.7 %copy-start.9 = (bf16[1536,384]{1,0:T(8,128)(2,1)S(1)}, bf16[1536,384]{1,0:T(8,128)(2,1)}, u32[]{:S(2)}) copy-start(bf16[1536,384]{1,0:T(8,128)(2,1)} %param.21) | copy-start | bytes 3538948
  7.2 48.1 %all-gather.3.cloned.1.call-start = ((), (), s32[]{:S(2)}) async-start(), calls=%async_computation.4 | async-start | bytes 1179648 | tf_op jit(solution)/shard_map/all_gather | solution.py:134
  13.0 92.7 %all-gather.5.cloned.1.call-start = ((), (), s32[]{:S(2)}) async-start(), calls=%async_computation.5 | async-start | bytes 2359296 | tf_op jit(solution)/shard_map/all_gather | solution.py:135
  13.9 172.4 %reduce-scatter.2.cloned.1.call-start = ((), (), s32[]{:S(2)}) async-start(), calls=%async_computation.6 | async-start | bytes 983040 | tf_op jit(solution)/shard_map/reduce_scatter | solution.py:164
  160.7 1.6 copy-start.5
  160.7 25.6 %copy-start.2 = (bf16[256,1536]{1,0:T(8,128)(2,1)S(1)}, bf16[256,1536]{1,0:T(8,128)(2,1)}, u32[]{:S(2)}) copy-start(bf16[256,1536]{1,0:T(8,128)(2,1)} %param.19) | copy-start | bytes 2359300
  160.7 26.7 %copy-start.7 = (f32[1536]{0:T(1024)S(1)}, f32[1536]{0:T(1024)}, u32[]{:S(2)}) copy-start(f32[1536]{0:T(1024)} %param.26) | copy-start | bytes 18436
  197.9 5.8 %copy-start.3 = (bf16[256,2,2,64]{0,3,2,1:T(8,128)(2,1)S(1)}, bf16[256,2,2,64]{0,3,2,1:T(8,128)(2,1)}, u32[]{:S(2)}) copy-start(bf16[256,2,2,64]{0,3,2,1:T(8,128)(2,1)} %pad_maximum_fusion) | copy-start | bytes 393220
  197.9 76.6 %all-to-all-start = ((bf16[8,4,32,1536]{3,2,1,0:T(8,128)(2,1)}), bf16[8,4,32,1536]{3,2,1,0:T(8,128)(2,1)}, u32[]{:S(2)}, u32[]{:S(2)}) async-start(bf16[8,4,32,1536]{3,2,1,0:T(8,128)(2,1)} %broadcast_select_fusion), calls=%async_computation.1 | async-start | bytes 6291456 | tf_op jit(solution)/shard_map/all_to_all | solution.py:198
  274.5 17.6 %all-to-all-start.2 = ((bf16[4,8,2048]{2,0,1:T(4,128)(2,1)}), bf16[4,8,2048]{2,0,1:T(4,128)(2,1)S(1)}, u32[]{:S(2)}, u32[]{:S(2)}) async-start(bf16[4,8,2048]{2,0,1:T(4,128)(2,1)} %copy.110), calls=%async_computation.3 | async-start | bytes 262144 | tf_op jit(solution)/shard_map/all_to_all | solution.py:92
  292.1 6.1 %copy-start.6 = (f32[64,8]{0,1:T(8,128)S(1)}, f32[64,8]{0,1:T(8,128)}, u32[]{:S(2)}) copy-start(f32[64,8]{0,1:T(8,128)} %param.30) | copy-start | bytes 6148
  292.1 7.1 %copy-start.8 = (s32[256]{0:T(256)S(1)}, s32[256]{0:T(256)}, u32[]{:S(2)}) copy-start(s32[256]{0:T(256)} %param.31) | copy-start | bytes 3076
  292.1 76.6 %all-to-all-start.1 = ((bf16[8,4,32,1536]{3,2,1,0:T(8,128)(2,1)}), bf16[8,4,32,1536]{3,2,1,0:T(8,128)(2,1)}, u32[]{:S(2)}, u32[]{:S(2)}) async-start(bf16[8,4,32,1536]{3,2,1,0:T(8,128)(2,1)} %copy.108), calls=%async_computation.2 | async-start | bytes 6291456 | tf_op jit(solution)/shard_map/all_to_all | solution.py:207
Sparse Core Ops, SparseCore 0:
  13.1 42.2 all-gather.2
  57.5 48.1 all-gather.4
  162.4 23.8 reduce-scatter.1
where the time goes:
time: 386 us; the launch traced here: 385 us
  waiting for transfers between devices  246 us (64%)
  local copies, waits for them, and re-layouts  49.6 us (13%)
  matrix products  28.3 us (7%)
  other arithmetic  28.1 us (7%)
  starting transfers between devices  15.7 us (4%)
  between operations  14.1 us (4%)
    all_to_all x1, waiting for transfers between devices, body(): lax.all_to_all(dispatched, 'seq', split_axis=0, concat_axis=0, tiled=True)  69.6 us
    all_to_all x1, waiting for transfers between devices, body(): lax.all_to_all(produced, 'seq', split_axis=0, concat_axis=0, tiled=True)  67.3 us
    all_gather x1, waiting for transfers between devices, body(): cache_piece = lax.all_gather(cache_lines, 'seq', axis=0, tiled=True)  49 us
    all_gather x1, waiting for transfers between devices, body(): new_piece = lax.all_gather(pairs_new, 'seq', axis=0, tiled=True)  40.6 us
    reduce_scatter x1, waiting for transfers between devices, body(): lax.psum_scatter(jnp.dot(attended, o_weight, preferred_element_type=jnp.f...  19.4 us
    unnamed x26, local copies, waits for them, and re-layouts  11.7 us
    reshape x1, local copies, waits for them, and re-layouts, body(): cache_piece.reshape(piece_rows // stride, 2 * stride, kv_local, 2, head_dim)  8.88 us
  transfers between devices with their start and end apart: 6, of which 5 were waited for; matrix products, arithmetic and copies ran while one was open for 7% of the time, Pallas kernels for 0%

commit v1 on v0

--- a/solution.py
+++ b/solution.py
@@ -132,7 +132,12 @@
 
     carried = start_state
     new_piece = lax.all_gather(pairs_new, "seq", axis=0, tiled=True)
-    cache_piece = lax.all_gather(cache_lines, "seq", axis=0, tiled=True)
+    ring = [cache_lines]
+    for hop in range(7):
+        ring.append(lax.ppermute(ring[-1], "seq", [(dev, (dev + 1) % 8) for dev in range(8)]))
+    cache_piece = jnp.roll(
+        jnp.concatenate(ring[::-1], axis=0), (lax.axis_index("seq") + 1) * ring[0].shape[0], axis=0
+    )
     piece_rows = new_piece.shape[0]
     stride = block_size(piece_rows)
     new_blocks = new_piece.reshape(piece_rows // stride, stride, -1)

time: 386 us -> 364 us (0.943)
  waiting for transfers between devices: 246 us -> 220 us
    ppermute x0 -> x7, waiting for transfers between devices: none -> 58.2 us  [body(): lax.ppermute(ring[-1], 'seq', [(dev, (dev + 1) % 8) for dev in range(8)])]
    all_gather x1 -> x0, waiting for transfers between devices: 49 us -> none  [body(): cache_piece = lax.all_gather(cache_lines, 'seq', axis=0, tiled=True)]
    all_gather x1, waiting for transfers between devices: 40.6 us -> 5.55 us  [body(): new_piece = lax.all_gather(pairs_new, 'seq', axis=0, tiled=True)]
    reshape x1, local copies, waits for them, and re-layouts: 8.88 us -> 3.66 us  [body(): cache_piece.reshape(piece_rows // stride, 2 * stride, kv_local, 2, head_dim)]
    unnamed x26 -> x37, local copies, waits for them, and re-layouts: 11.7 us -> 15.8 us
  transfers between devices with their start and end apart: 6 -> 12, of which waited for: 5 -> 11; matrix products, arithmetic and copies ran while one was open for 7% -> 14% of each run, Pallas kernels for 0% -> 0%
where the time goes in v1:
time: 364 us; the launch traced here: 363 us
  waiting for transfers between devices  220 us (60%)
  local copies, waits for them, and re-layouts  49.7 us (14%)
  matrix products  30.2 us (8%)
  other arithmetic  26.7 us (7%)
  starting transfers between devices  18.5 us (5%)
  between operations  14.5 us (4%)
    all_to_all x1, waiting for transfers between devices, body(): lax.all_to_all(dispatched, 'seq', split_axis=0, concat_axis=0, tiled=True)  69.6 us
    all_to_all x1, waiting for transfers between devices, body(): lax.all_to_all(produced, 'seq', split_axis=0, concat_axis=0, tiled=True)  67.3 us
    ppermute x7, waiting for transfers between devices, body(): lax.ppermute(ring[-1], 'seq', [(dev, (dev + 1) % 8) for dev in range(8)])  58.2 us
    reduce_scatter x1, waiting for transfers between devices, body(): lax.psum_scatter(jnp.dot(attended, o_weight, preferred_element_type=jnp.f...  19.8 us
    unnamed x37, local copies, waits for them, and re-layouts  15.8 us
    dot_general x1, matrix products, body(): jnp.einsum('sexd,edf->sexf', lax.all_to_all(dispatched, 'seq', split_axis...  7.37 us
  transfers between devices with their start and end apart: 12, of which 11 were waited for; matrix products, arithmetic and copies ran while one was open for 14% of the time, Pallas kernels for 0%

profile of v1, /device:TPU:0, one launch (start us, length us, event | category | flops | bytes accessed | tf_op | source)
XLA Modules:
  0.0 363.0 jit_solution(15823525190630028653)
XLA Ops:
  7.2 1.2 reshape.172
  8.4 3.0 collective-permute-start
  11.4 9.3 %collective-permute-done = bf16[256,512]{1,0:T(8,128)(2,1)S(1)} collective-permute-done((bf16[256,512]{1,0:T(8,128)(2,1)S(1)}, bf16[256,512]{1,0:T(8,128)(2,1)S(1)}, u32[]{:S(2)}, u32[]{:S(2)}) %collective-permute-start) | collective-permute-done | bytes 262176 | tf_op jit(solution)/shard_map/ppermute | solution.py:137
  20.8 10.2 %collective-permute-done.1 = bf16[256,512]{1,0:T(8,128)(2,1)S(1)} collective-permute-done((bf16[256,512]{1,0:T(8,128)(2,1)S(1)}, bf16[256,512]{1,0:T(8,128)(2,1)S(1)}, u32[]{:S(2)}, u32[]{:S(2)}) %collective-permute-start.1) | collective-permute-done | bytes 262176 | tf_op jit(solution)/shard_map/ppermute | solution.py:137
  30.9 9.3 %collective-permute-done.2 = bf16[256,512]{1,0:T(8,128)(2,1)S(1)} collective-permute-done((bf16[256,512]{1,0:T(8,128)(2,1)S(1)}, bf16[256,512]{1,0:T(8,128)(2,1)S(1)}, u32[]{:S(2)}, u32[]{:S(2)}) %collective-permute-start.2) | collective-permute-done | bytes 262176 | tf_op jit(solution)/shard_map/ppermute | solution.py:137
  40.2 1.4 fusion.45
  41.6 7.7 %collective-permute-done.3 = bf16[256,512]{1,0:T(8,128)(2,1)S(1)} collective-permute-done((bf16[256,512]{1,0:T(8,128)(2,1)S(1)}, bf16[256,512]{1,0:T(8,128)(2,1)S(1)}, u32[]{:S(2)}, u32[]{:S(2)}) %collective-permute-start.3) | collective-permute-done | bytes 262176 | tf_op jit(solution)/shard_map/ppermute | solution.py:137
  49.3 1.7 convolution_convert_fusion.3
  51.0 7.3 %collective-permute-done.4 = bf16[256,512]{1,0:T(8,128)(2,1)S(1)} collective-permute-done((bf16[256,512]{1,0:T(8,128)(2,1)S(1)}, bf16[256,512]{1,0:T(8,128)(2,1)S(1)}, u32[]{:S(2)}, u32[]{:S(2)}) %collective-permute-start.4) | collective-permute-done | bytes 262176 | tf_op jit(solution)/shard_map/ppermute | solution.py:137
  58.4 1.7 convolution_convert_fusion.2
  60.8 7.0 %collective-permute-done.5 = bf16[256,512]{1,0:T(8,128)(2,1)} collective-permute-done((bf16[256,512]{1,0:T(8,128)(2,1)S(1)}, bf16[256,512]{1,0:T(8,128)(2,1)}, u32[]{:S(2)}, u32[]{:S(2)}) %collective-permute-start.5) | collective-permute-done | bytes 262176 | tf_op jit(solution)/shard_map/ppermute | solution.py:137
  67.9 2.6 convolution_convert_fusion.1
  70.5 1.1 copy.99
  71.6 7.4 %collective-permute-done.6 = bf16[256,512]{1,0:T(8,128)(2,1)} collective-permute-done((bf16[256,512]{1,0:T(8,128)(2,1)}, bf16[256,512]{1,0:T(8,128)(2,1)}, u32[]{:S(2)}, u32[]{:S(2)}) %collective-permute-start.6) | collective-permute-done | bytes 262176 | tf_op jit(solution)/shard_map/ppermute | solution.py:137
  79.0 1.0 constant_dynamic-update-slice_fusion.15
  79.9 1.0 constant_dynamic-update-slice_fusion.14
  81.1 1.0 constant_dynamic-update-slice_fusion.7
  82.0 1.0 constant_dynamic-update-slice_fusion.6
  83.3 3.7 %reshape.173 = bf16[4,1024,2,2,64]{4,3,2,1,0:T(2,128)(2,1)} reshape(bf16[2048,512]{1,0:T(8,128)(2,1)S(1)} %constant_dynamic-slice_fusion.1) | data formatting | bytes 4194304 | tf_op jit(solution)/shard_map/reshape | solution.py:144
  87.0 10.7 %copy.101 = bf16[4,1024,2,2,64]{1,4,2,3,0:T(8,128)(2,1)} copy(bf16[4,1024,2,2,64]{4,3,2,1,0:T(2,128)(2,1)} %reshape.173) | data formatting | bytes 4194304
  97.6 5.5 %all-gather.2.cloned.1.call-done = bf16[2048,256]{0,1:T(8,128)(2,1)} async-done(((bf16[256,256]{0,1:T(8,128)(2,1)}), bf16[2048,256]{0,1:T(8,128)(2,1)}) %all-gather.2.cloned.1.call-update) | async-done | bytes 1048592 | tf_op jit(solution)/shard_map/all_gather | solution.py:134
  103.2 1.3 copy.142
  104.6 33.4 %while.16 = (s32[]{:T(128)}, f32[2,3,256]{2,1,0:T(4,128)S(1)}, f32[2,3,256]{2,1,0:T(4,128)S(1)}, f32[2,3,256,64]{2,3,1,0:T(8,128)S(1)}, pred[]{:T(512)}, /*index...) while((s32[]{:T(128)}, f32[2,3,256]{2,1,0:T(4,128)S(1)}, ...), condition=%wide.region_11.12_spmd.clone.clone, body=%wide.region_1.11_spmd.clone.clone.sunk | while | flops 627712256 | bytes 33374036 | solution.py:161
  107.8 2.5 conditional.8
  109.3 1.0 fusion.10
  110.3 4.5 %conditional.9 = ((f32[2,3,256]{2,1,0:T(4,128)S(1)}, f32[2,3,256]{2,1,0:T(4,128)S(1)}, f32[2,3,256,64]{2,3,1,0:T(8,128)S(1)})) conditional(s32[]{:T(128)} %convert_element_type.152, (f32[2,3,256]{2,1,0:T(4,128)S(1)}, f32[2,3,256]{2,1,0:T(4,128)S(1)}, f32[2,3,256,64]{2,3,1,0:T(8,128)S(1)}) %get-tuple-element.445, ...), branch_computations={%region_7.7_spmd, %region_8.10_spmd} | conditional | flops 415435776 | bytes 21532708 | solution.py:151
  110.3 1.1 dynamic-slice_bitcast_fusion
  111.4 1.0 bitcast_reduce_fusion
  112.5 1.0 fusion.19
  113.5 1.2 fusion.22
  118.0 4.5 %conditional.9 = ((f32[2,3,256]{2,1,0:T(4,128)S(1)}, f32[2,3,256]{2,1,0:T(4,128)S(1)}, f32[2,3,256,64]{2,3,1,0:T(8,128)S(1)})) conditional(s32[]{:T(128)} %convert_element_type.152, (f32[2,3,256]{2,1,0:T(4,128)S(1)}, f32[2,3,256]{2,1,0:T(4,128)S(1)}, f32[2,3,256,64]{2,3,1,0:T(8,128)S(1)}) %get-tuple-element.445, ...), branch_computations={%region_7.7_spmd, %region_8.10_spmd} | conditional | flops 415435776 | bytes 21532708 | solution.py:151
  118.0 1.1 dynamic-slice_bitcast_fusion
  119.1 1.0 bitcast_reduce_fusion
  120.2 1.0 fusion.19
  121.2 1.2 fusion.22
  125.8 4.5 %conditional.9 = ((f32[2,3,256]{2,1,0:T(4,128)S(1)}, f32[2,3,256]{2,1,0:T(4,128)S(1)}, f32[2,3,256,64]{2,3,1,0:T(8,128)S(1)})) conditional(s32[]{:T(128)} %convert_element_type.152, (f32[2,3,256]{2,1,0:T(4,128)S(1)}, f32[2,3,256]{2,1,0:T(4,128)S(1)}, f32[2,3,256,64]{2,3,1,0:T(8,128)S(1)}) %get-tuple-element.445, ...), branch_computations={%region_7.7_spmd, %region_8.10_spmd} | conditional | flops 415435776 | bytes 21532708 | solution.py:151
  125.8 1.1 dynamic-slice_bitcast_fusion
  126.9 1.0 bitcast_reduce_fusion
  127.9 1.0 fusion.19
  129.0 1.2 fusion.22
  133.5 4.5 %conditional.9 = ((f32[2,3,256]{2,1,0:T(4,128)S(1)}, f32[2,3,256]{2,1,0:T(4,128)S(1)}, f32[2,3,256,64]{2,3,1,0:T(8,128)S(1)})) conditional(s32[]{:T(128)} %convert_element_type.152, (f32[2,3,256]{2,1,0:T(4,128)S(1)}, f32[2,3,256]{2,1,0:T(4,128)S(1)}, f32[2,3,256,64]{2,3,1,0:T(8,128)S(1)}) %get-tuple-element.445, ...), branch_computations={%region_7.7_spmd, %region_8.10_spmd} | conditional | flops 415435776 | bytes 21532708 | solution.py:151
  133.5 1.1 dynamic-slice_bitcast_fusion
  134.6 1.0 bitcast_reduce_fusion
  135.7 1.0 fusion.19
  136.7 1.2 fusion.22
  138.1 1.5 convolution_convert_fusion
  139.9 1.2 reduce-window.6
  141.6 2.6 scatter_custom_fusion
  144.4 19.8 %reduce-scatter.2.cloned.1.call-done = bf16[64,1536]{1,0:T(8,128)(2,1)} async-done(((bf16[256,1536]{1,0:T(8,128)(2,1)}), bf16[64,1536]{1,0:T(8,128)(2,1)}) %reduce-scatter.2.cloned.1.call-update) | async-done | bytes 196624 | tf_op jit(solution)/shard_map/reduce_scatter | solution.py:169
  164.1 1.1 multiply_reduce_fusion
  165.3 1.0 multiply_convert_fusion
  166.3 5.6 %gather_fusion = bf16[1024,1536]{1,0:T(8,128)(2,1)} fusion(bf16[64,1536]{1,0:T(8,128)(2,1)S(1)} %multiply_convert_fusion, s32[1024]{0:T(1024)S(1)} %fusion.59), kind=kCustom, calls=%fused_computation | custom fusion | bytes 6295552 | tf_op jit(solution)/shard_map/gather | solution.py:197
  171.9 3.8 %broadcast_select_fusion = bf16[8,4,32,1536]{3,2,1,0:T(8,128)(2,1)} fusion(bf16[8,4,32,1536]{3,2,1,0:T(8,128)(2,1)} %bitcast.141, pred[8,4,32]{2,1,0:T(4,128)(4,1)S(1)} %broadcast_in_dim.86), kind=kLoop, calls=%fused_computation.51 | loop fusion | flops 1572864 | bytes 6292480 | tf_op jit(solution)/shard_map/jit(_where)/select_n | solution.py:198
  175.7 5.7 %all-to-all-start = ((bf16[8,4,32,1536]{3,2,1,0:T(8,128)(2,1)}), bf16[8,4,32,1536]{3,2,1,0:T(8,128)(2,1)}, u32[]{:S(2)}, u32[]{:S(2)}) async-start(bf16[8,4,32,1536]{3,2,1,0:T(8,128)(2,1)} %broadcast_select_fusion), calls=%async_computation.1 | async-start | bytes 6291456 | tf_op jit(solution)/shard_map/all_to_all | solution.py:203
  182.6 69.6 %all-to-all-done = bf16[8,4,32,1536]{3,2,1,0:T(8,128)(2,1)} async-done(((bf16[8,4,32,1536]{3,2,1,0:T(8,128)(2,1)}), bf16[8,4,32,1536]{3,2,1,0:T(8,128)(2,1)}, u32[]{:S(2)}, u32[]{:S(2)}) %all-to-all-start) | async-done | bytes 3145760 | tf_op jit(solution)/shard_map/all_to_all | solution.py:203
  252.2 3.6 %all-to-all-start.2 = ((bf16[4,8,2048]{2,0,1:T(4,128)(2,1)}), bf16[4,8,2048]{2,0,1:T(4,128)(2,1)S(1)}, u32[]{:S(2)}, u32[]{:S(2)}) async-start(bf16[4,8,2048]{2,0,1:T(4,128)(2,1)} %copy.110), calls=%async_computation.3 | async-start | bytes 262144 | tf_op jit(solution)/shard_map/all_to_all | solution.py:92
  255.8 7.4 %fusion.39 = f32[8,4,32,1024]{3,2,0,1:T(8,128)S(1)} fusion(bf16[4,1536,1024]{2,1,0:T(8,128)(2,1)} %param.27, bf16[8,4,32,1536]{3,2,1,0:T(8,128)(2,1)} %all-to-all-done), kind=kOutput, calls=%fused_computation.53 | convolution fusion | flops 3221225472 | bytes 19922944 | tf_op jit(solution)/shard_map/sexd,edf->sexf/dot_general | solution.py:201
  263.2 4.6 %fusion.34 = bf16[8,4,32,1536]{3,2,0,1:T(8,128)(2,1)S(1)} fusion(bf16[4,512,1536]{2,1,0:T(8,128)(2,1)} %param.28, f32[8,4,32,1024]{3,2,0,1:T(8,128)S(1)} %fusion.39), kind=kOutput, calls=%fused_computation.47 | convolution fusion | flops 1615331328 | bytes 13631488 | tf_op jit(solution)/shard_map/sexf,efd->sexd/dot_general | solution.py:209
  267.8 1.9 copy.108
  269.8 6.1 %all-to-all-start.1 = ((bf16[8,4,32,1536]{3,2,1,0:T(8,128)(2,1)}), bf16[8,4,32,1536]{3,2,1,0:T(8,128)(2,1)}, u32[]{:S(2)}, u32[]{:S(2)}) async-start(bf16[8,4,32,1536]{3,2,1,0:T(8,128)(2,1)} %copy.108), calls=%async_computation.2 | async-start | bytes 6291456 | tf_op jit(solution)/shard_map/all_to_all | solution.py:212
  279.0 67.3 %all-to-all-done.1 = bf16[8,4,32,1536]{3,2,1,0:T(8,128)(2,1)} async-done(((bf16[8,4,32,1536]{3,2,1,0:T(8,128)(2,1)}), bf16[8,4,32,1536]{3,2,1,0:T(8,128)(2,1)}, u32[]{:S(2)}, u32[]{:S(2)}) %all-to-all-start.1) | async-done | bytes 3145760 | tf_op jit(solution)/shard_map/all_to_all | solution.py:212
  346.3 5.9 %gather_fusion.1 = bf16[512,1536]{1,0:T(8,128)(2,1)S(1)} fusion(bf16[1024,1536]{1,0:T(8,128)(2,1)} %bitcast.33, s32[1024]{0:T(1024)S(1)} %pad_clamp_fusion), kind=kCustom, calls=%fused_computation.1 | custom fusion | bytes 3147776 | tf_op jit(solution)/shard_map/gather | solution.py:214
  352.2 2.2 fusion.37
  354.4 1.7 add_convert_fusion
  (131 shorter events, 18.6 us)
Async XLA Ops:
  7.2 130.9 %copy-start = (bf16[384,1536]{1,0:T(8,128)(2,1)S(1)}, bf16[384,1536]{1,0:T(8,128)(2,1)}, u32[]{:S(2)}) copy-start(bf16[384,1536]{1,0:T(8,128)(2,1)} %param.24) | copy-start | bytes 3538948
  7.2 60.7 %copy-start.1 = (bf16[256,1536]{1,0:T(8,128)(2,1)S(1)}, bf16[256,1536]{1,0:T(8,128)(2,1)}, u32[]{:S(2)}) copy-start(bf16[256,1536]{1,0:T(8,128)(2,1)} %param.19) | copy-start | bytes 2359300
  7.2 60.7 %copy-start.8 = (f32[1536]{0:T(1024)S(1)}, f32[1536]{0:T(1024)}, u32[]{:S(2)}) copy-start(f32[1536]{0:T(1024)} %param.20) | copy-start | bytes 18436
  7.2 96.0 %all-gather.2.cloned.1.call-start = ((), (), s32[]{:S(2)}) async-start(), calls=%async_computation.4 | async-start | bytes 1179648 | tf_op jit(solution)/shard_map/all_gather | solution.py:134
  8.4 12.3 %collective-permute-start = (bf16[256,512]{1,0:T(8,128)(2,1)S(1)}, bf16[256,512]{1,0:T(8,128)(2,1)S(1)}, u32[]{:S(2)}, u32[]{:S(2)}) collective-permute-start(bf16[256,512]{1,0:T(8,128)(2,1)S(1)} %reshape.172), channel_id=1, source_target_pairs={{0,4},{4,8},{8,12},{12,16},{16,20},{20,24},{24,28},{28,0},{1,5},{5... | collective-permute-start | bytes 786440 | tf_op jit(solution)/shard_map/ppermute | solution.py:137
  20.8 10.2 %collective-permute-start.1 = (bf16[256,512]{1,0:T(8,128)(2,1)S(1)}, bf16[256,512]{1,0:T(8,128)(2,1)S(1)}, u32[]{:S(2)}, u32[]{:S(2)}) collective-permute-start(bf16[256,512]{1,0:T(8,128)(2,1)S(1)} %collective-permute-done), channel_id=1, source_target_pairs={{0,4},{4,8},{8,12},{12,16},{16,20},{20,24},{24,28},{28,0},{1,5},{5... | collective-permute-start | bytes 786440 | tf_op jit(solution)/shard_map/ppermute | solution.py:137
  30.9 9.3 %collective-permute-start.2 = (bf16[256,512]{1,0:T(8,128)(2,1)S(1)}, bf16[256,512]{1,0:T(8,128)(2,1)S(1)}, u32[]{:S(2)}, u32[]{:S(2)}) collective-permute-start(bf16[256,512]{1,0:T(8,128)(2,1)S(1)} %collective-permute-done.1), channel_id=1, source_target_pairs={{0,4},{4,8},{8,12},{12,16},{16,20},{20,24},{24,28},{28,0},{1,5},{5... | collective-permute-start | bytes 786440 | tf_op jit(solution)/shard_map/ppermute | solution.py:137
  40.2 9.1 %collective-permute-start.3 = (bf16[256,512]{1,0:T(8,128)(2,1)S(1)}, bf16[256,512]{1,0:T(8,128)(2,1)S(1)}, u32[]{:S(2)}, u32[]{:S(2)}) collective-permute-start(bf16[256,512]{1,0:T(8,128)(2,1)S(1)} %collective-permute-done.2), channel_id=1, source_target_pairs={{0,4},{4,8},{8,12},{12,16},{16,20},{20,24},{24,28},{28,0},{1,5},{5... | collective-permute-start | bytes 786440 | tf_op jit(solution)/shard_map/ppermute | solution.py:137
  49.3 9.1 %collective-permute-start.4 = (bf16[256,512]{1,0:T(8,128)(2,1)S(1)}, bf16[256,512]{1,0:T(8,128)(2,1)S(1)}, u32[]{:S(2)}, u32[]{:S(2)}) collective-permute-start(bf16[256,512]{1,0:T(8,128)(2,1)S(1)} %collective-permute-done.3), channel_id=1, source_target_pairs={{0,4},{4,8},{8,12},{12,16},{16,20},{20,24},{24,28},{28,0},{1,5},{5... | collective-permute-start | bytes 786440 | tf_op jit(solution)/shard_map/ppermute | solution.py:137
  58.4 9.5 %collective-permute-start.5 = (bf16[256,512]{1,0:T(8,128)(2,1)S(1)}, bf16[256,512]{1,0:T(8,128)(2,1)}, u32[]{:S(2)}, u32[]{:S(2)}) collective-permute-start(bf16[256,512]{1,0:T(8,128)(2,1)S(1)} %collective-permute-done.4), channel_id=1, source_target_pairs={{0,4},{4,8},{8,12},{12,16},{16,20},{20,24},{24,28},{28,0},{1,5},{5... | collective-permute-start | bytes 786440 | tf_op jit(solution)/shard_map/ppermute | solution.py:137
  60.8 103.3 %reduce-scatter.2.cloned.1.call-start = ((), (), s32[]{:S(2)}) async-start(), calls=%async_computation.5 | async-start | bytes 983040 | tf_op jit(solution)/shard_map/reduce_scatter | solution.py:169
  67.9 11.1 %collective-permute-start.6 = (bf16[256,512]{1,0:T(8,128)(2,1)}, bf16[256,512]{1,0:T(8,128)(2,1)}, u32[]{:S(2)}, u32[]{:S(2)}) collective-permute-start(bf16[256,512]{1,0:T(8,128)(2,1)} %collective-permute-done.5), channel_id=1, source_target_pairs={{0,4},{4,8},{8,12},{12,16},{16,20},{20,24},{24,28},{28,0},{1,5},{5... | collective-permute-start | bytes 786440 | tf_op jit(solution)/shard_map/ppermute | solution.py:137
  138.0 1.6 copy-start.4
  138.0 26.1 %copy-start.2 = (bf16[256,1536]{1,0:T(8,128)(2,1)S(1)}, bf16[256,1536]{1,0:T(8,128)(2,1)}, u32[]{:S(2)}) copy-start(bf16[256,1536]{1,0:T(8,128)(2,1)} %param.19) | copy-start | bytes 2359300
  138.0 27.2 %copy-start.6 = (f32[1536]{0:T(1024)S(1)}, f32[1536]{0:T(1024)}, u32[]{:S(2)}) copy-start(f32[1536]{0:T(1024)} %param.26) | copy-start | bytes 18436
  175.7 5.7 %copy-start.3 = (bf16[256,2,2,64]{0,3,2,1:T(8,128)(2,1)S(1)}, bf16[256,2,2,64]{0,3,2,1:T(8,128)(2,1)}, u32[]{:S(2)}) copy-start(bf16[256,2,2,64]{0,3,2,1:T(8,128)(2,1)} %pad_maximum_fusion) | copy-start | bytes 393220
  175.7 76.5 %all-to-all-start = ((bf16[8,4,32,1536]{3,2,1,0:T(8,128)(2,1)}), bf16[8,4,32,1536]{3,2,1,0:T(8,128)(2,1)}, u32[]{:S(2)}, u32[]{:S(2)}) async-start(bf16[8,4,32,1536]{3,2,1,0:T(8,128)(2,1)} %broadcast_select_fusion), calls=%async_computation.1 | async-start | bytes 6291456 | tf_op jit(solution)/shard_map/all_to_all | solution.py:203
  252.2 17.6 %all-to-all-start.2 = ((bf16[4,8,2048]{2,0,1:T(4,128)(2,1)}), bf16[4,8,2048]{2,0,1:T(4,128)(2,1)S(1)}, u32[]{:S(2)}, u32[]{:S(2)}) async-start(bf16[4,8,2048]{2,0,1:T(4,128)(2,1)} %copy.110), calls=%async_computation.3 | async-start | bytes 262144 | tf_op jit(solution)/shard_map/all_to_all | solution.py:92
  269.8 6.1 %copy-start.5 = (f32[64,8]{0,1:T(8,128)S(1)}, f32[64,8]{0,1:T(8,128)}, u32[]{:S(2)}) copy-start(f32[64,8]{0,1:T(8,128)} %param.30) | copy-start | bytes 6148
  269.8 7.1 %copy-start.7 = (s32[256]{0:T(256)S(1)}, s32[256]{0:T(256)}, u32[]{:S(2)}) copy-start(s32[256]{0:T(256)} %param.31) | copy-start | bytes 3076
  269.8 76.6 %all-to-all-start.1 = ((bf16[8,4,32,1536]{3,2,1,0:T(8,128)(2,1)}), bf16[8,4,32,1536]{3,2,1,0:T(8,128)(2,1)}, u32[]{:S(2)}, u32[]{:S(2)}) async-start(bf16[8,4,32,1536]{3,2,1,0:T(8,128)(2,1)} %copy.108), calls=%async_computation.2 | async-start | bytes 6291456 | tf_op jit(solution)/shard_map/all_to_all | solution.py:212
Sparse Core Ops, SparseCore 0:
  60.9 42.2 all-gather.1
  139.7 24.3 reduce-scatter.1
